TPU v7x, 512 devices: a whole 4x8x8 slice. The times are simulated.
512 devices in a mesh: req: 64 (over y, x, core), tp: 8 (over z).
Axes of the slice: x: 4, y: 8, z: 8, core: 2. Of those that a mesh axis runs over, the one named last changes fastest.
Arguments:
- tokens: bfloat16 [8192, 8192], P('req', 'tp'), may hold values from -6 to 6
- kv_weight: bfloat16 [8192, 1024], P('tp'), may hold values from -0.0625 to 0.0625
- queries: bfloat16 [8192, 4096], P('req', 'tp'), may hold values from -96 to 96, as said below
- lengths: int32 [32], replicated, may hold values from 1 to 384, 8192 in all
- page_owner: int32 [4096, 1], P('req'), may hold values from 0 to 63; in each aligned block of 64 rows (0 to 63, 64 to 127, ...) at most 2 rows name the same one
Outputs:
- attended: bfloat16 [8192, 4096], P('req', 'tp')
- cache: bfloat16 [16384, 1024], P('req', 'tp')
Inputs may be any that keep to these rules, and one draw needn't show every extreme that they name: `queries`: real values; entries of a row share a scale. The 32 lengths sum to 8192; the largest is exactly 384. `page_owner`: among the 64 pages of one device no owner is named more than 2 times, a bound that some block reaches.
All inputs are finite; a program needn't handle non-finite values.
Results may differ from a plain program's by a relative error of at most 0.012.
Values may be sent and summed in bfloat16 or wider, within the bound.
No kernel may reach another device: no remote copies, remote signals or barrier semaphores. Data moves between devices by JAX's collectives and lax.ppermute only.
A program may use at most 64 MiB of HBM per device.

v0:
```python
import math

import jax
import jax.numpy as jnp
from jax import lax
from jax.sharding import PartitionSpec as P


HD = 128
BACK = 3


rope_base = 500000.0


def shifted(value, axis, steps):
    count = lax.axis_size(axis)
    first, last = (max(0, -steps), min(count, count - steps))
    return lax.ppermute(value, axis, [(source, source + steps) for source in range(first, last)])


def rotate(values, positions):
    middle = HD // 2
    frequency = rope_base ** (-(2.0 * jnp.arange(middle, dtype=jnp.float32)) / HD)
    angles = positions.astype(jnp.float32)[:, None] * frequency[None, :]
    cosine = jnp.cos(angles)[:, None, :]
    sine = jnp.sin(angles)[:, None, :]
    front = values[..., :middle]
    behind = values[..., middle:]
    return jnp.concatenate(
        [front * cosine - behind * sine, behind * cosine + front * sine], axis=-1
    )


def segment_info(lengths, indices):
    ends = jnp.cumsum(lengths)
    before = ends[None, :] <= indices[:, None]
    segment = jnp.sum(before.astype(jnp.int32), axis=1)
    start = jnp.sum(jnp.where(before, lengths[None, :], 0), axis=1)
    return (segment, indices - start)


def layer(tokens, kv_weight, queries, lengths, page_owner):
    rows = tokens.shape[0]
    tp_size = lax.axis_size("tp")
    tp_index = lax.axis_index("tp")
    req_index = lax.axis_index("req")
    local_index = req_index * rows + jnp.arange(rows, dtype=jnp.int32)
    segment, positions = segment_info(lengths, local_index)
    local_heads = queries.shape[1] // HD
    partial_value = jnp.dot(tokens, kv_weight, preferred_element_type=jnp.float32)
    heads_here = partial_value.shape[1] // (2 * HD)
    per_head = tp_size // heads_here
    half = rows // per_head
    parts = partial_value.reshape(rows, heads_here, 2, HD)
    key_high = lax.optimization_barrier(parts[:, :, 0, :].astype(jnp.bfloat16))
    key_low = (parts[:, :, 0, :] - key_high.astype(jnp.float32)).astype(jnp.bfloat16)
    value_high = parts[:, :, 1, :].astype(jnp.bfloat16)
    packed = jnp.concatenate([key_high, key_low, value_high], axis=2)
    packed = jnp.transpose(packed.reshape(per_head, half, heads_here, 3 * HD), (2, 0, 1, 3))
    arrived = lax.all_to_all(packed.reshape(tp_size, half, 3 * HD), "tp", 0, 0, tiled=True)
    arrived = jnp.sum(arrived.astype(jnp.float32), axis=0)
    side = tp_index % per_head
    key_sum = arrived[:, :HD] + arrived[:, HD : 2 * HD]
    here = lax.dynamic_slice_in_dim(positions, side * half, half, 0)
    key_now = rotate(key_sum.reshape(half, 1, HD), here).reshape(half, HD)
    finished = jnp.concatenate([key_now, arrived[:, 2 * HD :]], axis=1).astype(jnp.bfloat16)
    other = lax.ppermute(finished, "tp", [(i, i ^ 1) for i in range(tp_size)])
    first = side == 0
    near = jnp.concatenate([jnp.where(first, finished, other), jnp.where(first, other, finished)], axis=0)
    mine = lax.dynamic_slice_in_dim(near, side * HD, HD, 1)
    rotated = rotate(queries.astype(jnp.float32).reshape(rows, local_heads, HD), positions).astype(
        jnp.bfloat16
    )
    blocks = []
    for distance in range(BACK, 0, -1):
        blocks.append(shifted(near, "req", distance))
    blocks.append(near)
    window = jnp.concatenate(blocks, axis=0)
    key_total = (BACK + 1) * rows
    key_index = (req_index - BACK) * rows + jnp.arange(key_total, dtype=jnp.int32)
    key_segment, _ = segment_info(lengths, key_index)
    allowed = (
        (key_index[None, :] >= 0)
        & (key_index[None, :] <= local_index[:, None])
        & (key_segment[None, :] == segment[:, None])
    )
    key_head = window[:, :HD]
    value_head = window[:, HD:]
    scores = lax.dot_general(
        rotated, key_head, (((2,), (1,)), ((), ())), preferred_element_type=jnp.float32
    ) / math.sqrt(HD)
    scores = jnp.where(allowed[:, None, :], scores, -1e30)
    largest = jnp.max(scores, axis=2, keepdims=True)
    weights = jnp.exp(scores - largest)
    total = jnp.sum(weights, axis=2, keepdims=True)
    mixed = lax.dot_general(
        weights.astype(jnp.bfloat16), value_head, (((2,), (0,)), ((), ())),
        preferred_element_type=jnp.float32,
    )
    attended = (mixed / total).astype(jnp.bfloat16).reshape(rows, local_heads * HD)
    pages_here = page_owner.shape[0]
    owners = page_owner[:, 0]
    page_rows = rows // pages_here
    capacity = 2 * pages_here // lax.axis_size("req")
    order = jnp.arange(pages_here, dtype=jnp.int32)
    earlier = (owners[:, None] == owners[None, :]) & (order[None, :] < order[:, None])
    rank = jnp.sum(earlier.astype(jnp.int32), axis=1)
    target = owners * capacity + rank
    slots = lax.axis_size("req") * capacity
    row_target = (target[:, None] * page_rows + jnp.arange(page_rows, dtype=jnp.int32)[None, :]).reshape(rows)
    placing = (jnp.arange(slots * page_rows, dtype=jnp.int32)[:, None] == row_target[None, :]).astype(jnp.bfloat16)
    outgoing = jnp.dot(placing, mine, preferred_element_type=jnp.float32).astype(jnp.bfloat16)
    cache = lax.all_to_all(outgoing, "req", 0, 0, tiled=True)
    return (attended, cache)


def solution(mesh):
    in_specs = (P("req", "tp"), P("tp", None), P("req", "tp"), P(), P("req", None))
    out_specs = (P("req", "tp"), P("req", "tp"))
    return jax.shard_map(layer, mesh=mesh, in_specs=in_specs, out_specs=out_specs, check_vma=False)
```

profile of v0, /device:TPU:1, one launch (start us, length us, event | category | flops | bytes accessed | tf_op | source)
XLA Modules:
  0.0 68.3 jit_solution(10365043169766177543)
XLA Ops:
  0.6 0.0 copy-start
  0.6 1.6 %copy-done = bf16[1024,1024]{1,0:T(8,128)(2,1)S(1)} copy-done((bf16[1024,1024]{1,0:T(8,128)(2,1)S(1)}, bf16[1024,1024]{1,0:T(8,128)(2,1)}, u32[]{:S(2)}) %copy-start) | copy-done | bytes 2097176
  2.2 1.4 %fusion.36 = f32[128,1024]{1,0:T(8,128)S(1)} fusion(bf16[128,1024]{1,0:T(8,128)(2,1)} %param.5, bf16[1024,1024]{1,0:T(8,128)(2,1)S(1)} %copy-done), kind=kOutput, calls=%fused_computation.78 | convolution fusion | flops 268435456 | bytes 2883584 | tf_op jit(solution)/shard_map/dot_general | solution.py:51
  3.6 0.4 reshape.294
  4.1 0.0 copy-start.3
  4.1 0.0 copy-start.2
  4.1 0.0 copy-start.1
  4.1 0.2 slice.49
  4.3 0.3 slice.50
  4.7 0.8 %pad_maximum_fusion = bf16[128,4,384]{2,0,1:T(8,128)(2,1)} fusion(bf16[128,4,128]{2,0,1:T(8,128)(2,1)S(1)} %bitcast.47, bf16[128,4,128]{2,0,1:T(8,128)(2,1)S(1)} %subtract_convert_fusion, bf16[128,4,128]{2,0,1:T(8,128)(2,1)S(1)} %bitcast.46), kind=kLoop, calls=%fused_computation.10 | loop fusion | flops 1179648 | bytes 786432 | tf_op jit(solution)/shard_map/concatenate | solution.py:59
  5.5 10.9 %all-to-all-start = ((bf16[8,64,384]{2,1,0:T(8,128)(2,1)}), bf16[8,64,384]{2,1,0:T(8,128)(2,1)S(1)}, u32[]{:S(2)}, u32[]{:S(2)}) async-start(bf16[8,64,384]{2,1,0:T(8,128)(2,1)} %bitcast.7), calls=%async_computation | async-start | bytes 786432 | tf_op jit(solution)/shard_map/all_to_all | solution.py:61
  16.4 0.0 copy-done.3
  16.4 0.2 convert_reduce_fusion.2
  16.6 0.1 copy.19
  16.7 0.1 reduce-window.8
  16.7 0.1 reduce
  16.9 0.1 fusion.25
  17.0 0.1 convert_reduce_fusion.1
  17.1 0.0 copy-done.1
  17.1 0.1 copy.20
  17.2 0.1 copy.30
  17.4 0.1 copy.29
  17.5 0.1 dynamic-slice_convert_fusion
  17.6 0.1 compare_and_fusion
  17.7 0.3 multiply_cosine_fusion
  18.0 0.1 subtract_convert_fusion.1
  18.1 12.5 %all-to-all-done = bf16[8,64,384]{2,1,0:T(8,128)(2,1)S(1)} async-done(((bf16[8,64,384]{2,1,0:T(8,128)(2,1)}), bf16[8,64,384]{2,1,0:T(8,128)(2,1)S(1)}, u32[]{:S(2)}, u32[]{:S(2)}) %all-to-all-start) | async-done | bytes 393248 | tf_op jit(solution)/shard_map/all_to_all | solution.py:61
  30.6 0.1 convert_reduce_fusion
  30.7 0.2 fusion.17
  30.9 0.1 maximum_bitcast_fusion
  31.0 1.9 %collective-permute-start = (bf16[64,256]{1,0:T(8,128)(2,1)S(1)}, bf16[64,256]{1,0:T(8,128)(2,1)S(1)}, u32[]{:S(2)}, u32[]{:S(2)}) collective-permute-start(bf16[64,256]{1,0:T(8,128)(2,1)S(1)} %pad_maximum_fusion.2), channel_id=1, source_target_pairs={{0,1},{1,0},{2,3},{3,2},{4,5},{5,4},{6,7},{7,6},{8,9},{9,8},{10,11... | collective-permute-start | bytes 98312 | tf_op jit(solution)/shard_map/ppermute | solution.py:68
  32.9 0.1 iota_add_fusion
  33.0 0.1 add.90
  33.1 2.5 %collective-permute-done = bf16[64,256]{1,0:T(8,128)(2,1)S(1)} collective-permute-done((bf16[64,256]{1,0:T(8,128)(2,1)S(1)}, bf16[64,256]{1,0:T(8,128)(2,1)S(1)}, u32[]{:S(2)}, u32[]{:S(2)}) %collective-permute-start) | collective-permute-done | bytes 32800 | tf_op jit(solution)/shard_map/ppermute | solution.py:68
  35.7 5.5 %collective-permute-start.3 = (bf16[128,256]{1,0:T(8,128)(2,1)S(1)}, bf16[128,256]{1,0:T(8,128)(2,1)S(1)}, u32[]{:S(2)}, u32[]{:S(2)}) collective-permute-start(bf16[128,256]{1,0:T(8,128)(2,1)S(1)} %pad_maximum_fusion.1), channel_id=1, source_target_pairs={{0,8},{8,16},{16,24},{24,32},{32,40},{40,48},{48,56},{56,64},{64,7... | collective-permute-start | bytes 196616 | tf_op jit(solution)/shard_map/ppermute | solution.py:19
  41.2 3.1 %collective-permute-start.2 = (bf16[128,256]{1,0:T(8,128)(2,1)S(1)}, bf16[128,256]{1,0:T(8,128)(2,1)S(1)}, u32[]{:S(2)}, u32[]{:S(2)}) collective-permute-start(bf16[128,256]{1,0:T(8,128)(2,1)S(1)} %pad_maximum_fusion.1), channel_id=1, source_target_pairs={{0,16},{8,24},{16,32},{24,40},{32,48},{40,56},{48,64},{56,72},{64,... | collective-permute-start | bytes 196616 | tf_op jit(solution)/shard_map/ppermute | solution.py:19
  44.3 3.4 %collective-permute-start.1 = (bf16[128,256]{1,0:T(8,128)(2,1)S(1)}, bf16[128,256]{1,0:T(8,128)(2,1)S(1)}, u32[]{:S(2)}, u32[]{:S(2)}) collective-permute-start(bf16[128,256]{1,0:T(8,128)(2,1)S(1)} %pad_maximum_fusion.1), channel_id=1, source_target_pairs={{0,24},{8,32},{16,40},{24,48},{32,56},{40,64},{48,72},{56,80},{64,... | collective-permute-start | bytes 196616 | tf_op jit(solution)/shard_map/ppermute | solution.py:19
  47.8 0.8 %convolution_convert_fusion = bf16[256,128]{1,0:T(8,128)(2,1)} fusion(s32[128]{0:T(128)S(1)} %add.90, s32[]{:T(128)S(6)} %select_n.40, bf16[64,256]{1,0:T(8,128)(2,1)S(1)} %get-tuple-element.16, bf16[64,256]{1,0:T(8,128)(2,1)S(1)} %get-tuple-element.17), kind=kOutput, calls=%fused_computation.4 | convolution fusion | flops 8519680 | bytes 131588 | tf_op jit(solution)/shard_map/dot_general | solution.py:113
  48.6 9.0 %all-to-all-start.1 = ((bf16[64,4,128]{2,1,0:T(4,128)(2,1)}), bf16[64,4,128]{2,1,0:T(4,128)(2,1)S(1)}, u32[]{:S(2)}, u32[]{:S(2)}) async-start(bf16[64,4,128]{2,1,0:T(4,128)(2,1)} %bitcast.16), calls=%async_computation.1 | async-start | bytes 131072 | tf_op jit(solution)/shard_map/all_to_all | solution.py:114
  57.6 0.0 collective-permute-done.1
  57.6 0.0 collective-permute-done.2
  57.7 0.0 collective-permute-done.3
  57.7 0.5 fusion.35
  58.2 0.3 fusion.2
  58.5 0.5 fusion.1
  59.0 0.8 %copy.26 = bf16[128,512]{1,0:T(8,128)(2,1)} copy(bf16[128,512]{0,1:T(8,128)(2,1)S(1)} %bitcast.49) | data formatting | bytes 262144
  59.7 8.0 %all-to-all-done.1 = bf16[64,4,128]{2,1,0:T(4,128)(2,1)S(1)} async-done(((bf16[64,4,128]{2,1,0:T(4,128)(2,1)}), bf16[64,4,128]{2,1,0:T(4,128)(2,1)S(1)}, u32[]{:S(2)}, u32[]{:S(2)}) %all-to-all-start.1) | async-done | bytes 65568 | tf_op jit(solution)/shard_map/all_to_all | solution.py:114
  67.7 0.6 copy.48
  (21 shorter events, 0.2 us)
Async XLA Ops:
  0.6 1.6 %copy-start = (bf16[1024,1024]{1,0:T(8,128)(2,1)S(1)}, bf16[1024,1024]{1,0:T(8,128)(2,1)}, u32[]{:S(2)}) copy-start(bf16[1024,1024]{1,0:T(8,128)(2,1)} %param.6) | copy-start | bytes 6291460
  4.1 12.3 %copy-start.3 = (s32[64,1]{0,1:T(1,128)S(1)}, s32[64,1]{0,1:T(1,128)}, u32[]{:S(2)}) copy-start(s32[64,1]{0,1:T(1,128)} %param.9) | copy-start | bytes 772
  4.1 12.5 %copy-start.2 = (s32[32]{0:T(128)S(1)}, s32[32]{0:T(128)}, u32[]{:S(2)}) copy-start(s32[32]{0:T(128)} %param.8) | copy-start | bytes 388
  4.1 13.0 %copy-start.1 = (bf16[128,512]{1,0:T(8,128)(2,1)S(1)}, bf16[128,512]{1,0:T(8,128)(2,1)}, u32[]{:S(2)}) copy-start(bf16[128,512]{1,0:T(8,128)(2,1)} %param.7) | copy-start | bytes 393220
  5.5 25.1 %all-to-all-start = ((bf16[8,64,384]{2,1,0:T(8,128)(2,1)}), bf16[8,64,384]{2,1,0:T(8,128)(2,1)S(1)}, u32[]{:S(2)}, u32[]{:S(2)}) async-start(bf16[8,64,384]{2,1,0:T(8,128)(2,1)} %bitcast.7), calls=%async_computation | async-start | bytes 786432 | tf_op jit(solution)/shard_map/all_to_all | solution.py:61
  31.0 4.7 %collective-permute-start = (bf16[64,256]{1,0:T(8,128)(2,1)S(1)}, bf16[64,256]{1,0:T(8,128)(2,1)S(1)}, u32[]{:S(2)}, u32[]{:S(2)}) collective-permute-start(bf16[64,256]{1,0:T(8,128)(2,1)S(1)} %pad_maximum_fusion.2), channel_id=1, source_target_pairs={{0,1},{1,0},{2,3},{3,2},{4,5},{5,4},{6,7},{7,6},{8,9},{9,8},{10,11... | collective-permute-start | bytes 98312 | tf_op jit(solution)/shard_map/ppermute | solution.py:68
  35.7 22.0 %collective-permute-start.3 = (bf16[128,256]{1,0:T(8,128)(2,1)S(1)}, bf16[128,256]{1,0:T(8,128)(2,1)S(1)}, u32[]{:S(2)}, u32[]{:S(2)}) collective-permute-start(bf16[128,256]{1,0:T(8,128)(2,1)S(1)} %pad_maximum_fusion.1), channel_id=1, source_target_pairs={{0,8},{8,16},{16,24},{24,32},{32,40},{40,48},{48,56},{56,64},{64,7... | collective-permute-start | bytes 196616 | tf_op jit(solution)/shard_map/ppermute | solution.py:19
  41.2 16.4 %collective-permute-start.2 = (bf16[128,256]{1,0:T(8,128)(2,1)S(1)}, bf16[128,256]{1,0:T(8,128)(2,1)S(1)}, u32[]{:S(2)}, u32[]{:S(2)}) collective-permute-start(bf16[128,256]{1,0:T(8,128)(2,1)S(1)} %pad_maximum_fusion.1), channel_id=1, source_target_pairs={{0,16},{8,24},{16,32},{24,40},{32,48},{40,56},{48,64},{56,72},{64,... | collective-permute-start | bytes 196616 | tf_op jit(solution)/shard_map/ppermute | solution.py:19
  44.3 13.3 %collective-permute-start.1 = (bf16[128,256]{1,0:T(8,128)(2,1)S(1)}, bf16[128,256]{1,0:T(8,128)(2,1)S(1)}, u32[]{:S(2)}, u32[]{:S(2)}) collective-permute-start(bf16[128,256]{1,0:T(8,128)(2,1)S(1)} %pad_maximum_fusion.1), channel_id=1, source_target_pairs={{0,24},{8,32},{16,40},{24,48},{32,56},{40,64},{48,72},{56,80},{64,... | collective-permute-start | bytes 196616 | tf_op jit(solution)/shard_map/ppermute | solution.py:19
  48.6 19.1 %all-to-all-start.1 = ((bf16[64,4,128]{2,1,0:T(4,128)(2,1)}), bf16[64,4,128]{2,1,0:T(4,128)(2,1)S(1)}, u32[]{:S(2)}, u32[]{:S(2)}) async-start(bf16[64,4,128]{2,1,0:T(4,128)(2,1)} %bitcast.16), calls=%async_computation.1 | async-start | bytes 131072 | tf_op jit(solution)/shard_map/all_to_all | solution.py:114
where the time goes:
time: 68.7 us; the launch traced here: 68.3 us
  starting transfers between devices  33.9 us (49%)
  waiting for transfers between devices  23 us (33%)
  local copies, waits for them, and re-layouts  4.61 us (7%)
  matrix products  3.1 us (5%)
  other arithmetic  2.76 us (4%)
  between operations  1.02 us (1%)
    all_to_all x1, waiting for transfers between devices, layer(): lax.all_to_all(packed.reshape(tp_size, half, 3 * HD), 'tp', 0, 0, tiled=T...  12.5 us
    ppermute x3, starting transfers between devices, shifted(): lax.ppermute(value, axis, [(source, source + steps) for source in range(f...  12.1 us
    all_to_all x1, starting transfers between devices, layer(): lax.all_to_all(packed.reshape(tp_size, half, 3 * HD), 'tp', 0, 0, tiled=T...  10.9 us
    all_to_all x1, starting transfers between devices, layer(): cache = lax.all_to_all(outgoing, 'req', 0, 0, tiled=True)  9.02 us
    all_to_all x1, waiting for transfers between devices, layer(): cache = lax.all_to_all(outgoing, 'req', 0, 0, tiled=True)  7.95 us
    unnamed x19, local copies, waits for them, and re-layouts  3.46 us
    ppermute x1, waiting for transfers between devices, layer(): other = lax.ppermute(finished, 'tp', [(i, i ^ 1) for i in range(tp_size)])  2.51 us
    ppermute x1, starting transfers between devices, layer(): other = lax.ppermute(finished, 'tp', [(i, i ^ 1) for i in range(tp_size)])  1.92 us
  transfers between devices with their start and end apart: 6, of which 3 were waited for; matrix products, arithmetic and copies ran while one was open for 7% of the time, Pallas kernels for 0%

commit v1 on v0

--- a/solution.py
+++ b/solution.py
@@ -52,19 +52,23 @@
     heads_here = partial_value.shape[1] // (2 * HD)
     per_head = tp_size // heads_here
     half = rows // per_head
-    parts = partial_value.reshape(rows, heads_here, 2, HD)
-    key_high = lax.optimization_barrier(parts[:, :, 0, :].astype(jnp.bfloat16))
-    key_low = (parts[:, :, 0, :] - key_high.astype(jnp.float32)).astype(jnp.bfloat16)
-    value_high = parts[:, :, 1, :].astype(jnp.bfloat16)
-    packed = jnp.concatenate([key_high, key_low, value_high], axis=2)
-    packed = jnp.transpose(packed.reshape(per_head, half, heads_here, 3 * HD), (2, 0, 1, 3))
-    arrived = lax.all_to_all(packed.reshape(tp_size, half, 3 * HD), "tp", 0, 0, tiled=True)
+    high = lax.optimization_barrier(partial_value.astype(jnp.bfloat16))
+    low = (partial_value - high.astype(jnp.float32)).astype(jnp.bfloat16)
+    chunks = []
+    for head in range(heads_here):
+        for part in range(per_head):
+            lines = slice(part * half, (part + 1) * half)
+            chunks.append(jnp.concatenate([
+                high[lines, head * 2 * HD : (head + 1) * 2 * HD],
+                low[lines, head * 2 * HD : head * 2 * HD + HD],
+            ], axis=1))
+    arrived = lax.all_to_all(jnp.stack(chunks), "tp", 0, 0, tiled=True)
     arrived = jnp.sum(arrived.astype(jnp.float32), axis=0)
     side = tp_index % per_head
-    key_sum = arrived[:, :HD] + arrived[:, HD : 2 * HD]
+    key_sum = arrived[:, :HD] + arrived[:, 2 * HD :]
     here = lax.dynamic_slice_in_dim(positions, side * half, half, 0)
     key_now = rotate(key_sum.reshape(half, 1, HD), here).reshape(half, HD)
-    finished = jnp.concatenate([key_now, arrived[:, 2 * HD :]], axis=1).astype(jnp.bfloat16)
+    finished = jnp.concatenate([key_now, arrived[:, HD : 2 * HD]], axis=1).astype(jnp.bfloat16)
     other = lax.ppermute(finished, "tp", [(i, i ^ 1) for i in range(tp_size)])
     first = side == 0
     near = jnp.concatenate([jnp.where(first, finished, other), jnp.where(first, other, finished)], axis=0)

time: 68.7 us -> 72 us (1.048)
  other arithmetic: 2.76 us -> 6.94 us
  local copies, waits for them, and re-layouts: 4.61 us -> 3.71 us
    unnamed x0 -> x7, other arithmetic: none -> 4.34 us
    concatenate x2 -> x1, other arithmetic: 0.8 us -> 0.01 us  [layer(): jnp.concatenate([key_now, arrived[:, HD:2 * HD]], axis=1)]
    unnamed x19 -> x17, local copies, waits for them, and re-layouts: 3.46 us -> 3.41 us
where the time goes in v1:
time: 72 us; the launch traced here: 71.6 us
  starting transfers between devices  33.9 us (47%)
  waiting for transfers between devices  22.9 us (32%)
  other arithmetic  6.94 us (10%)
  local copies, waits for them, and re-layouts  3.71 us (5%)
  matrix products  3.11 us (4%)
  between operations  1 us (1%)
    all_to_all x1, waiting for transfers between devices, layer(): arrived = lax.all_to_all(jnp.stack(chunks), 'tp', 0, 0, tiled=True)  12.5 us
    ppermute x3, starting transfers between devices, shifted(): lax.ppermute(value, axis, [(source, source + steps) for source in range(f...  12.1 us
    all_to_all x1, starting transfers between devices, layer(): arrived = lax.all_to_all(jnp.stack(chunks), 'tp', 0, 0, tiled=True)  10.9 us
    all_to_all x1, starting transfers between devices, layer(): cache = lax.all_to_all(outgoing, 'req', 0, 0, tiled=True)  9.02 us
    all_to_all x1, waiting for transfers between devices, layer(): cache = lax.all_to_all(outgoing, 'req', 0, 0, tiled=True)  7.95 us
    unnamed x7, other arithmetic  4.34 us
    unnamed x17, local copies, waits for them, and re-layouts  3.41 us
    ppermute x1, waiting for transfers between devices, layer(): other = lax.ppermute(finished, 'tp', [(i, i ^ 1) for i in range(tp_size)])  2.51 us
  transfers between devices with their start and end apart: 6, of which 3 were waited for; matrix products, arithmetic and copies ran while one was open for 7% of the time, Pallas kernels for 0%

profile of v1, /device:TPU:1, one launch (start us, length us, event | category | flops | bytes accessed | tf_op | source)
XLA Modules:
  0.0 71.6 jit_solution(17186655734316555976)
XLA Ops:
  0.6 0.0 copy-start
  0.6 1.6 %copy-done = bf16[1024,1024]{1,0:T(8,128)(2,1)S(1)} copy-done((bf16[1024,1024]{1,0:T(8,128)(2,1)S(1)}, bf16[1024,1024]{1,0:T(8,128)(2,1)}, u32[]{:S(2)}) %copy-start) | copy-done | bytes 2097176
  2.2 1.4 %fusion.43 = (bf16[128,1024]{1,0:T(8,128)(2,1)S(1)}, f32[128,1024]{1,0:T(8,128)S(1)}) fusion(bf16[128,1024]{1,0:T(8,128)(2,1)} %param.5, bf16[1024,1024]{1,0:T(8,128)(2,1)S(1)} %copy-done), kind=kOutput, calls=%fused_computation.90 | convolution fusion | flops 268566528 | bytes 3145728 | tf_op jit(solution)/shard_map/dot_general | solution.py:51
  3.6 0.0 copy-start.3
  3.6 0.0 copy-start.2
  3.7 0.0 copy-start.1
  3.7 0.1 subtract_convert_fusion
  3.8 0.6 fusion.10
  4.4 0.6 fusion.11
  5.0 0.6 fusion.12
  5.7 0.6 fusion.13
  6.3 0.6 fusion.14
  6.9 0.6 fusion.15
  7.5 0.6 fusion.16
  8.1 0.6 fusion.17
  8.7 10.9 %all-to-all-start = ((bf16[8,64,384]{2,1,0:T(8,128)(2,1)}), bf16[8,64,384]{2,1,0:T(8,128)(2,1)S(1)}, u32[]{:S(2)}, u32[]{:S(2)}) async-start(bf16[8,64,384]{2,1,0:T(8,128)(2,1)} %fusion.17), calls=%async_computation | async-start | bytes 786432 | tf_op jit(solution)/shard_map/all_to_all | solution.py:65
  19.7 0.2 convert_reduce_fusion.2
  19.9 0.1 copy.16
  20.0 0.1 reduce-window.8
  20.0 0.1 reduce
  20.1 0.1 fusion.31
  20.2 0.1 convert_reduce_fusion.1
  20.3 0.1 copy.17
  20.5 0.1 copy.25
  20.6 0.1 copy.24
  20.8 0.1 dynamic-slice_convert_fusion
  20.8 0.1 compare_and_fusion
  21.0 0.3 multiply_cosine_fusion
  21.3 0.1 subtract_convert_fusion.1
  21.4 12.5 %all-to-all-done = bf16[8,64,384]{2,1,0:T(8,128)(2,1)S(1)} async-done(((bf16[8,64,384]{2,1,0:T(8,128)(2,1)}), bf16[8,64,384]{2,1,0:T(8,128)(2,1)S(1)}, u32[]{:S(2)}, u32[]{:S(2)}) %all-to-all-start) | async-done | bytes 393248 | tf_op jit(solution)/shard_map/all_to_all | solution.py:65
  33.9 0.1 convert_reduce_fusion
  34.0 0.2 fusion.23
  34.2 0.1 maximum_bitcast_fusion.8
  34.2 1.9 %collective-permute-start = (bf16[64,256]{1,0:T(8,128)(2,1)S(1)}, bf16[64,256]{1,0:T(8,128)(2,1)S(1)}, u32[]{:S(2)}, u32[]{:S(2)}) collective-permute-start(bf16[64,256]{1,0:T(8,128)(2,1)S(1)} %pad_maximum_fusion.1), channel_id=1, source_target_pairs={{0,1},{1,0},{2,3},{3,2},{4,5},{5,4},{6,7},{7,6},{8,9},{9,8},{10,11... | collective-permute-start | bytes 98312 | tf_op jit(solution)/shard_map/ppermute | solution.py:72
  36.2 0.1 iota_add_fusion
  36.2 0.1 add.90
  36.4 2.5 %collective-permute-done = bf16[64,256]{1,0:T(8,128)(2,1)S(1)} collective-permute-done((bf16[64,256]{1,0:T(8,128)(2,1)S(1)}, bf16[64,256]{1,0:T(8,128)(2,1)S(1)}, u32[]{:S(2)}, u32[]{:S(2)}) %collective-permute-start) | collective-permute-done | bytes 32800 | tf_op jit(solution)/shard_map/ppermute | solution.py:72
  38.9 5.5 %collective-permute-start.3 = (bf16[128,256]{1,0:T(8,128)(2,1)S(1)}, bf16[128,256]{1,0:T(8,128)(2,1)S(1)}, u32[]{:S(2)}, u32[]{:S(2)}) collective-permute-start(bf16[128,256]{1,0:T(8,128)(2,1)S(1)} %pad_maximum_fusion), channel_id=1, source_target_pairs={{0,8},{8,16},{16,24},{24,32},{32,40},{40,48},{48,56},{56,64},{64,7... | collective-permute-start | bytes 196616 | tf_op jit(solution)/shard_map/ppermute | solution.py:19
  44.5 3.1 %collective-permute-start.2 = (bf16[128,256]{1,0:T(8,128)(2,1)S(1)}, bf16[128,256]{1,0:T(8,128)(2,1)S(1)}, u32[]{:S(2)}, u32[]{:S(2)}) collective-permute-start(bf16[128,256]{1,0:T(8,128)(2,1)S(1)} %pad_maximum_fusion), channel_id=1, source_target_pairs={{0,16},{8,24},{16,32},{24,40},{32,48},{40,56},{48,64},{56,72},{64,... | collective-permute-start | bytes 196616 | tf_op jit(solution)/shard_map/ppermute | solution.py:19
  47.6 3.4 %collective-permute-start.1 = (bf16[128,256]{1,0:T(8,128)(2,1)S(1)}, bf16[128,256]{1,0:T(8,128)(2,1)S(1)}, u32[]{:S(2)}, u32[]{:S(2)}) collective-permute-start(bf16[128,256]{1,0:T(8,128)(2,1)S(1)} %pad_maximum_fusion), channel_id=1, source_target_pairs={{0,24},{8,32},{16,40},{24,48},{32,56},{40,64},{48,72},{56,80},{64,... | collective-permute-start | bytes 196616 | tf_op jit(solution)/shard_map/ppermute | solution.py:19
  51.0 0.8 %convolution_convert_fusion = bf16[256,128]{1,0:T(8,128)(2,1)} fusion(s32[128]{0:T(128)S(1)} %add.90, s32[]{:T(128)S(6)} %select_n.40, bf16[64,256]{1,0:T(8,128)(2,1)S(1)} %get-tuple-element.32, bf16[64,256]{1,0:T(8,128)(2,1)S(1)} %get-tuple-element.33), kind=kOutput, calls=%fused_computation.4 | convolution fusion | flops 8519680 | bytes 131588 | tf_op jit(solution)/shard_map/dot_general | solution.py:117
  51.8 9.0 %all-to-all-start.1 = ((bf16[64,4,128]{2,1,0:T(4,128)(2,1)}), bf16[64,4,128]{2,1,0:T(4,128)(2,1)S(1)}, u32[]{:S(2)}, u32[]{:S(2)}) async-start(bf16[64,4,128]{2,1,0:T(4,128)(2,1)} %bitcast.19), calls=%async_computation.1 | async-start | bytes 131072 | tf_op jit(solution)/shard_map/all_to_all | solution.py:118
  61.0 0.5 fusion.44
  61.4 0.3 fusion.2
  61.8 0.5 fusion.1
  62.2 0.8 %copy.21 = bf16[128,512]{1,0:T(8,128)(2,1)} copy(bf16[128,512]{0,1:T(8,128)(2,1)S(1)} %bitcast.63) | data formatting | bytes 262144
  63.0 7.9 %all-to-all-done.1 = bf16[64,4,128]{2,1,0:T(4,128)(2,1)S(1)} async-done(((bf16[64,4,128]{2,1,0:T(4,128)(2,1)}), bf16[64,4,128]{2,1,0:T(4,128)(2,1)S(1)}, u32[]{:S(2)}, u32[]{:S(2)}) %all-to-all-start.1) | async-done | bytes 65568 | tf_op jit(solution)/shard_map/all_to_all | solution.py:118
  71.0 0.6 copy.38
  (25 shorter events, 0.2 us)
Async XLA Ops:
  0.6 1.6 %copy-start = (bf16[1024,1024]{1,0:T(8,128)(2,1)S(1)}, bf16[1024,1024]{1,0:T(8,128)(2,1)}, u32[]{:S(2)}) copy-start(bf16[1024,1024]{1,0:T(8,128)(2,1)} %param.6) | copy-start | bytes 6291460
  3.6 16.0 %copy-start.3 = (s32[64,1]{0,1:T(1,128)S(1)}, s32[64,1]{0,1:T(1,128)}, u32[]{:S(2)}) copy-start(s32[64,1]{0,1:T(1,128)} %param.9) | copy-start | bytes 772
  3.6 16.2 %copy-start.2 = (s32[32]{0:T(128)S(1)}, s32[32]{0:T(128)}, u32[]{:S(2)}) copy-start(s32[32]{0:T(128)} %param.8) | copy-start | bytes 388
  3.7 16.7 %copy-start.1 = (bf16[128,512]{1,0:T(8,128)(2,1)S(1)}, bf16[128,512]{1,0:T(8,128)(2,1)}, u32[]{:S(2)}) copy-start(bf16[128,512]{1,0:T(8,128)(2,1)} %param.7) | copy-start | bytes 393220
  8.7 25.1 %all-to-all-start = ((bf16[8,64,384]{2,1,0:T(8,128)(2,1)}), bf16[8,64,384]{2,1,0:T(8,128)(2,1)S(1)}, u32[]{:S(2)}, u32[]{:S(2)}) async-start(bf16[8,64,384]{2,1,0:T(8,128)(2,1)} %fusion.17), calls=%async_computation | async-start | bytes 786432 | tf_op jit(solution)/shard_map/all_to_all | solution.py:65
  34.2 4.7 %collective-permute-start = (bf16[64,256]{1,0:T(8,128)(2,1)S(1)}, bf16[64,256]{1,0:T(8,128)(2,1)S(1)}, u32[]{:S(2)}, u32[]{:S(2)}) collective-permute-start(bf16[64,256]{1,0:T(8,128)(2,1)S(1)} %pad_maximum_fusion.1), channel_id=1, source_target_pairs={{0,1},{1,0},{2,3},{3,2},{4,5},{5,4},{6,7},{7,6},{8,9},{9,8},{10,11... | collective-permute-start | bytes 98312 | tf_op jit(solution)/shard_map/ppermute | solution.py:72
  38.9 22.0 %collective-permute-start.3 = (bf16[128,256]{1,0:T(8,128)(2,1)S(1)}, bf16[128,256]{1,0:T(8,128)(2,1)S(1)}, u32[]{:S(2)}, u32[]{:S(2)}) collective-permute-start(bf16[128,256]{1,0:T(8,128)(2,1)S(1)} %pad_maximum_fusion), channel_id=1, source_target_pairs={{0,8},{8,16},{16,24},{24,32},{32,40},{40,48},{48,56},{56,64},{64,7... | collective-permute-start | bytes 196616 | tf_op jit(solution)/shard_map/ppermute | solution.py:19
  44.5 16.4 %collective-permute-start.2 = (bf16[128,256]{1,0:T(8,128)(2,1)S(1)}, bf16[128,256]{1,0:T(8,128)(2,1)S(1)}, u32[]{:S(2)}, u32[]{:S(2)}) collective-permute-start(bf16[128,256]{1,0:T(8,128)(2,1)S(1)} %pad_maximum_fusion), channel_id=1, source_target_pairs={{0,16},{8,24},{16,32},{24,40},{32,48},{40,56},{48,64},{56,72},{64,... | collective-permute-start | bytes 196616 | tf_op jit(solution)/shard_map/ppermute | solution.py:19
  47.6 13.3 %collective-permute-start.1 = (bf16[128,256]{1,0:T(8,128)(2,1)S(1)}, bf16[128,256]{1,0:T(8,128)(2,1)S(1)}, u32[]{:S(2)}, u32[]{:S(2)}) collective-permute-start(bf16[128,256]{1,0:T(8,128)(2,1)S(1)} %pad_maximum_fusion), channel_id=1, source_target_pairs={{0,24},{8,32},{16,40},{24,48},{32,56},{40,64},{48,72},{56,80},{64,... | collective-permute-start | bytes 196616 | tf_op jit(solution)/shard_map/ppermute | solution.py:19
  51.8 19.1 %all-to-all-start.1 = ((bf16[64,4,128]{2,1,0:T(4,128)(2,1)}), bf16[64,4,128]{2,1,0:T(4,128)(2,1)S(1)}, u32[]{:S(2)}, u32[]{:S(2)}) async-start(bf16[64,4,128]{2,1,0:T(4,128)(2,1)} %bitcast.19), calls=%async_computation.1 | async-start | bytes 131072 | tf_op jit(solution)/shard_map/all_to_all | solution.py:118
